TPU v7x, 32 devices: a whole 2x2x4 slice. The times are simulated.
32 devices in a mesh: groups: 2 (over x), visit: 8 (over z, y), tile: 2 (over core).
Axes of the slice: x: 2, y: 2, z: 4, core: 2. Of those that a mesh axis runs over, the one named last changes fastest.
Arguments:
- exposure: float32 [16, 512, 2048], P(('groups', 'visit'), 'tile'), parts along dimension 0, may hold values from -12 to 12, as said below
- partners: int32 [16, 8], P('groups'), parts along dimension 0, may hold values from 0 to 7, as said below
- offsets: int32 [16, 8], P('groups'), parts along dimension 0, may hold values from -32 to 32
- stamps: int32 [16, 2, 8, 2], P(('groups', 'visit'), 'tile'), parts along dimension 0, may hold values from 0 to 1920, as said below
Outputs:
- difference: float32 [16, 512, 2048], P(('groups', 'visit'), 'tile'), parts along dimension 0
- coefficients: float32 [16, 33], P(('groups', 'visit')), parts along dimension 0
There are 2 independent parts, one for each index of `groups`. A program takes and returns all parts, laid end to end along the dimension named above; each array names one. Nothing has to cross between parts.
Inputs may be any that keep to these rules, and one draw needn't show every extreme that they name: Every row of partners names each of the 8 visits once, and so does every column. `stamps`: A stamp's row anchor lies in 0..128, its column anchor in 0..1920. `exposure`: images of order one.
All inputs are finite; a program needn't handle non-finite values.
Results may differ from a plain program's by a relative error of at most 0.0003.
Values sent between devices are 32-bit elements; how exact they have to be, the bound alone decides.
No kernel may reach another device: no remote copies, remote signals or barrier semaphores. Data moves between devices by JAX's collectives and lax.ppermute only.
A program may use at most 128 MiB of HBM per device.

v0:
```python
import jax
import jax.numpy as jnp
from jax import lax
from jax.sharding import PartitionSpec as P

STAMP = 128
KERNEL = 31
TERMS = 11
SHIFT = 32


RIDGE = 0.05
SIGMA_LIST = (1.0, 1.0, 1.0, 2.0, 2.0, 4.0)
POWER_LIST = (0, 1, 2, 0, 1, 0)
ALL_FILTERS = (0, 1, 2, 3, 4, 5)
COLUMN_PICK = (0, 1, 0, 2, 1, 0, 3, 4, 3, 5)
ROW_PICK = (0, 0, 1, 0, 1, 2, 3, 3, 4, 5)


def extended_2(block, sides, width):
    for axis, dim in sides:
        count = lax.axis_size(axis)
        forward = [(i, i + 1) for i in range(count - 1)]
        backward = [(target, source) for source, target in forward]
        low = lax.ppermute(
            lax.slice_in_dim(block, block.shape[dim] - width, None, axis=dim), axis, forward
        )
        high = lax.ppermute(lax.slice_in_dim(block, 0, width, axis=dim), axis, backward)
        block = jnp.concatenate([low, block, high], axis=dim)
    return block


def profiles():
    taps = (jnp.arange(KERNEL) - KERNEL // 2).astype(jnp.float32)
    stacked = []
    for sigma, power in zip(SIGMA_LIST, POWER_LIST):
        bell = jnp.exp(-taps * taps / (2.0 * sigma * sigma))
        stacked.append(bell * (taps / sigma) ** power / jnp.sum(bell))
    return jnp.stack(stacked)


def coordinates(count, first, total):
    return (
        2.0 * (first + jnp.arange(count, dtype=jnp.int32)).astype(jnp.float32) + 1.0
    ) / total - 1.0


def band(table, picks, count):
    spans = (
        jnp.arange(count + KERNEL - 1, dtype=jnp.int32)[:, None]
        - jnp.arange(count, dtype=jnp.int32)[None, :]
    )
    inside = (spans >= 0) & (spans < KERNEL)
    clipped = jnp.clip(spans, 0, KERNEL - 1)
    chosen = table[jnp.array(picks, dtype=jnp.int32)]
    return jnp.where(inside[None], chosen[:, clipped], 0.0)


def convolve(patch, across, downward):
    spread = jnp.einsum("yq,fqo->yfo", patch, across, precision=lax.Precision.HIGHEST)
    picked = spread[:, jnp.array(COLUMN_PICK, dtype=jnp.int32), :]
    return jnp.einsum("kqy,qkc->kyc", downward, picked, precision=lax.Precision.HIGHEST)


def design_sums(images, science, row_coord, col_coord):
    ones = jnp.ones((row_coord.shape[0], col_coord.shape[0]), jnp.float32)
    poly = jnp.stack([ones, ones * col_coord[None, :], ones * row_coord[:, None]])
    terms = (images[:, None] * poly[None]).reshape(30, -1)
    design = jnp.concatenate([terms, poly.reshape(3, -1)], axis=0)
    gram = jnp.dot(design, design.T, precision=lax.Precision.HIGHEST)
    vector = jnp.dot(design, science.reshape(-1), precision=lax.Precision.HIGHEST)
    return (gram, vector)


def solve_fit(gram, vector):
    regular = gram + RIDGE * jnp.diag(jnp.diag(gram))
    lower = jnp.linalg.cholesky(regular)
    return jax.scipy.linalg.cho_solve((lower, True), vector)


def model_of(images, solution, row_coord, col_coord):
    weights = solution[:30].reshape(10, 3)
    scale = (
        weights[:, 0, None, None]
        + weights[:, 1, None, None] * col_coord[None, None, :]
        + weights[:, 2, None, None] * row_coord[None, :, None]
    )
    background = (
        solution[30] + solution[31] * col_coord[None, :] + solution[32] * row_coord[:, None]
    )
    return jnp.sum(images * scale, axis=0) + background


def shards(exposure, partners, offsets, stamps):
    visits = lax.axis_size("visit")
    tiles = lax.axis_size("tile")
    my_visit = lax.axis_index("visit")
    my_tile = lax.axis_index("tile")
    image = exposure[0]
    height = image.shape[0]
    width = image.shape[1]
    block = height // visits
    blocks = image.reshape(visits, block, width)
    my_sources = lax.dynamic_slice_in_dim(partners, my_visit, 1, 0)[0]
    my_amounts = lax.dynamic_slice_in_dim(offsets, my_visit, 1, 0)[0]
    piece = lax.all_gather(blocks[None], "visit", axis=0, tiled=True)
    owners = jnp.arange(piece.shape[0], dtype=jnp.int32)

    def add_owner(owner_index, total):
        wanted = owners[owner_index] == my_sources
        return total + jnp.where(wanted[:, None, None], piece[owner_index], 0.0)

    assembled = lax.fori_loop(0, piece.shape[0], add_owner, jnp.zeros_like(blocks))
    padded_cols = jnp.pad(assembled, ((0, 0), (0, 0), (SHIFT, SHIFT)))

    def shift_block(rows_block, amount):
        return lax.dynamic_slice_in_dim(rows_block, SHIFT + amount, width, 1)

    template = jax.vmap(shift_block)(padded_cols, my_amounts).reshape(height, width)
    half = KERNEL // 2
    extended = extended_2(template, (("tile", 0),), half)
    field = jnp.pad(extended, ((0, 0), (half, half)))
    table = profiles()
    row_coord = coordinates(height, my_tile * height, height * tiles)
    col_coord = coordinates(width, 0, width)
    stamp_across = band(table, ALL_FILTERS, STAMP)
    stamp_down = band(table, ROW_PICK, STAMP)

    def add_stamp(carry, anchor):
        row_start = anchor[0]
        col_start = anchor[1]
        patch = lax.dynamic_slice(
            field, (row_start, col_start), (STAMP + 2 * half, STAMP + 2 * half)
        )
        images = convolve(patch, stamp_across, stamp_down)
        science_cut = lax.dynamic_slice(image, (row_start, col_start), (STAMP, STAMP))
        row_part = lax.dynamic_slice_in_dim(row_coord, row_start, STAMP)
        col_part = lax.dynamic_slice_in_dim(col_coord, col_start, STAMP)
        gram_term, vector_term = design_sums(images, science_cut, row_part, col_part)
        return ((carry[0] + gram_term, carry[1] + vector_term), None)

    start = (jnp.zeros((3 * TERMS, 3 * TERMS), jnp.float32), jnp.zeros((3 * TERMS,), jnp.float32))
    (gram, vector), _ = lax.scan(add_stamp, start, stamps[0, 0])
    gram, vector = lax.psum((gram, vector), "tile")
    solution = solve_fit(gram, vector)
    across = band(table, ALL_FILTERS, 128)
    row_blocks = height // STAMP
    col_blocks = width // 128

    def image_block(block_index):
        row_start = block_index // col_blocks * STAMP
        col_start = block_index % col_blocks * 128
        patch = lax.dynamic_slice(field, (row_start, col_start), (STAMP + 2 * half, 128 + 2 * half))
        images = convolve(patch, across, stamp_down)
        row_part = lax.dynamic_slice_in_dim(row_coord, row_start, STAMP)
        col_part = lax.dynamic_slice_in_dim(col_coord, col_start, 128)
        science_cut = lax.dynamic_slice(image, (row_start, col_start), (STAMP, 128))
        return science_cut - model_of(images, solution, row_part, col_part)

    pieces = lax.map(image_block, jnp.arange(row_blocks * col_blocks, dtype=jnp.int32))
    pieces = pieces.reshape(row_blocks, col_blocks, STAMP, 128)
    difference = jnp.transpose(pieces, (0, 2, 1, 3)).reshape(height, width)
    return (difference[None], solution[None])


def solution(mesh):
    return jax.shard_map(
        shards,
        mesh=mesh,
        in_specs=(
            P(("groups", "visit"), "tile", None),
            P("groups", None),
            P("groups", None),
            P(("groups", "visit"), "tile", None, None),
        ),
        out_specs=(P(("groups", "visit"), "tile", None), P(("groups", "visit"), None)),
        check_vma=False,
    )
```

profile of v0, /device:TPU:0, one launch (start us, length us, event | category | flops | bytes accessed | tf_op | source)
XLA Modules:
  0.0 918.3 jit_solution(15050697580024253793)
XLA Ops:
  13.1 37.8 %gather_fusion.5 = f32[20224,10]{1,0:T(8,128)} fusion(f32[10,31]{0,1:T(8,128)S(1)} %copy.28, s32[20480]{0:T(1024)S(1)} %pad_clamp_fusion.2), kind=kCustom, calls=%fused_computation.5 | custom fusion | bytes 1698816 | tf_op jit(solution)/shard_map/gather | solution.py:56
  50.9 6.8 copy.29
  58.4 37.8 %gather_fusion.3 = f32[20224,6]{1,0:T(8,128)} fusion(f32[6,31]{0,1:T(8,128)S(1)} %copy.26, s32[20480]{0:T(1024)S(1)} %pad_clamp_fusion.2), kind=kCustom, calls=%fused_computation.3 | custom fusion | bytes 1051648 | tf_op jit(solution)/shard_map/gather | solution.py:56
  96.2 7.2 copy.27
  105.4 135.1 %all-gather.2.cloned.1.call-done = f32[8,8,32,2048]{3,2,1,0:T(8,128)} async-done(((f32[1,8,32,2048]{3,2,1,0:T(8,128)}), f32[8,8,32,2048]{3,2,1,0:T(8,128)}) %all-gather.2.cloned.1.call-update) | async-done | bytes 16777232 | tf_op jit(solution)/shard_map/all_gather | solution.py:106
  240.5 27.8 %while.44 = (s32[]{:T(128)}, f32[8,32,2048]{2,1,0:T(8,128)S(1)}, s32[8]{0:T(128)S(1)}, s32[8]{0:T(128)S(1)}, f32[8,8,32,2048]{3,2,1,0:T(8,128)}, /*index=5*/s32[]{:T(128)}, s32[]{:T(128)}) while((s32[]{:T(128)}, f32[8,32,2048]{2,1,0:T(8,128)S(1)}, s32[8]{0:T(128)S(1)}, s32[8]{0:T(128)S(1)}, f32[8,8,32,2048]{3,2,1,0:T(8,128)}, ...), condition=%wide.region_1.2_spmd.clone, body=%wide.region_0.1_spmd.clone.sunk | while | flops 1572875 | bytes 6291611 | solution.py:113
  270.4 30.2 %while.42 = (s32[]{:T(128)}, f32[8,32,2112]{2,1,0:T(8,128)}, s32[8,3]{0,1:T(4,128)S(1)}, f32[8,32,2048]{2,1,0:T(8,128)}, s32[]{:T(128)}) while((s32[]{:T(128)}, f32[8,32,2112]{2,1,0:T(8,128)}, s32[8,3]{0,1:T(4,128)S(1)}, f32[8,32,2048]{2,1,0:T(8,128)}, s32[]{:T(128)}) %tuple.124), condition=%wide.while_cond, body=%wide.while_body.sunk | while | flops 2 | bytes 525929 | solution.py:117
  271.0 3.1 dynamic-slice_dynamic-update-slice_fusion.2
  274.8 3.1 dynamic-slice_dynamic-update-slice_fusion.2
  278.6 3.1 dynamic-slice_dynamic-update-slice_fusion.2
  282.4 3.1 dynamic-slice_dynamic-update-slice_fusion.2
  286.1 3.1 dynamic-slice_dynamic-update-slice_fusion.2
  289.9 3.1 dynamic-slice_dynamic-update-slice_fusion.2
  293.7 3.1 dynamic-slice_dynamic-update-slice_fusion.2
  297.5 3.1 dynamic-slice_dynamic-update-slice_fusion.2
  306.2 3.8 select_maximum_fusion
  310.0 177.0 %while.45 = (s32[]{:T(128)}, f32[33,33]{1,0:T(8,128)S(1)}, f32[33]{0:T(128)S(1)}, s32[8,2]{0,1:T(2,128)S(1)}, f32[286,2078]{1,0:T(8,128)}, /*index=5*/f32[6,158,...) while((s32[]{:T(128)}, f32[33,33]{1,0:T(8,128)S(1)}, ...), condition=%wide.region_6.7_spmd.clone.clone, body=%wide.region_5.6_spmd.sunk.clone.clone.sunk | while | flops 762977472 | bytes 24572200 | solution.py:143
  326.5 3.2 fusion.75
  348.6 3.2 fusion.75
  370.8 3.2 fusion.75
  392.9 3.2 fusion.75
  415.0 3.2 fusion.75
  437.2 3.2 fusion.75
  459.3 3.2 fusion.75
  481.4 3.2 fusion.75
  486.9 3.7 all-reduce.3
  491.9 3.0 cholesky.16
  496.3 2.5 custom-call.10
  499.2 408.5 %while.43 = (s32[]{:T(128)}, f32[32,128,128]{1,2,0:T(8,128)}, s32[32]{0:T(128)S(1)}, f32[256,2048]{1,0:T(8,128)}, f32[286,2078]{1,0:T(8,128)}, /*index=5*/f32[6,...) while((s32[]{:T(128)}, f32[32,128,128]{1,2,0:T(8,128)}, ...), condition=%wide.region_13.14_spmd.clone, body=%wide.region_11.13_spmd.sunk.clone.sunk | while | flops 541238400 | bytes 4926202 | solution.py:160
  508.0 2.3 fusion.65
  520.7 2.3 fusion.65
  546.3 2.3 fusion.65
  (733 shorter events, 462.7 us)
Async XLA Ops:
  7.2 96.2 %copy-start = (s32[8,8]{1,0:T(8,128)S(1)}, s32[8,8]{1,0:T(8,128)}, u32[]{:S(2)}) copy-start(s32[8,8]{1,0:T(8,128)} %param.16) | copy-start | bytes 772
  7.2 5.2 copy-start.7
  7.2 233.3 %all-gather.2.cloned.1.call-start = ((), (), s32[]{:S(2)}) async-start(), calls=%async_computation | async-start | bytes 18874368 | tf_op jit(solution)/shard_map/all_gather | solution.py:106
  301.6 2.9 collective-permute-start
  302.9 3.2 collective-permute-start.1
  304.4 5.5 copy-start.5
  304.5 5.5 copy-start.6
  323.5 1.2 copy-start.3
  326.5 3.2 copy-start.2
  345.5 1.2 copy-start.3
  348.6 3.2 copy-start.2
  367.7 1.2 copy-start.3
  370.7 3.2 copy-start.2
  389.8 1.2 copy-start.3
  392.9 3.2 copy-start.2
  411.9 1.2 copy-start.3
  415.0 3.2 copy-start.2
  434.1 1.2 copy-start.3
  437.1 3.2 copy-start.2
  456.2 1.2 copy-start.3
  459.3 3.2 copy-start.2
  478.3 1.2 copy-start.3
  481.4 3.2 copy-start.2
  907.7 2.3 copy-start.4
  910.0 1.5 copy-start.1
Sparse Core Ops, SparseCore 0:
  10.2 230.3 all-gather.1
where the time goes:
time: 925 us; the launch traced here: 918 us
  local copies, waits for them, and re-layouts  275 us (30%)
  matrix products  198 us (21%)
  loops' own time  146 us (16%)
  other arithmetic  141 us (15%)
  waiting for transfers between devices  137 us (15%)
  between operations  14.3 us (2%)
    all_gather x1, waiting for transfers between devices, shards(): piece = lax.all_gather(blocks[None], 'visit', axis=0, tiled=True)  135 us
    dot_general x40, matrix products, convolve(): jnp.einsum('kqy,qkc->kyc', downward, picked, precision=lax.Precision.HIGH...  92 us
    another operation x1, loops' own time, shards(): lax.map(image_block, jnp.arange(row_blocks * col_blocks, dtype=jnp.int32))  91.6 us
    gather x4, local copies, waits for them, and re-layouts, band(): return jnp.where(inside[None], chosen[:, clipped], 0.0)  89.5 us
    add x32, other arithmetic, model_of(): solution[30] + solution[31] * col_coord[None, :]  65 us
    dot_general x40, matrix products, convolve(): jnp.einsum('yq,fqo->yfo', patch, across, precision=lax.Precision.HIGHEST)  62.2 us
    another operation x1, loops' own time, shards(): (gram, vector), _ = lax.scan(add_stamp, start, stamps[0, 0])  54 us
    gather x24, local copies, waits for them, and re-layouts  30.2 us
  transfers between devices with their start and end apart: 3, of which 2 were waited for; matrix products, arithmetic and copies ran while one was open for 11% of the time, Pallas kernels for 0%

commit v1 on v0

v1 whole, which is shorter than its diff:
```python
import numpy as np
import jax
import jax.numpy as jnp
from jax import lax
from jax.sharding import PartitionSpec as P

STAMP = 128
KERNEL = 31
HALF = KERNEL // 2
TERMS = 11
SHIFT = 32
LANE = 128
HI = lax.Precision.HIGHEST


RIDGE = 0.05
SIGMA_LIST = (1.0, 1.0, 1.0, 2.0, 2.0, 4.0)
POWER_LIST = (0, 1, 2, 0, 1, 0)
COLUMN_PICK = (0, 1, 0, 2, 1, 0, 3, 4, 3, 5)
ROW_PICK = (0, 0, 1, 0, 1, 2, 3, 3, 4, 5)


def profile_table():
    taps = np.arange(KERNEL, dtype=np.float64) - HALF
    stacked = []
    for sigma, power in zip(SIGMA_LIST, POWER_LIST):
        bell = np.exp(-taps * taps / (2.0 * sigma * sigma))
        stacked.append(bell * (taps / sigma) ** power / np.sum(bell))
    return np.stack(stacked)


def column_bands(table):
    spans = np.arange(2 * LANE)[:, None] - np.arange(LANE)[None, :]
    inside = (spans >= 0) & (spans < KERNEL)
    picked = table[:, np.clip(spans, 0, KERNEL - 1)]
    return np.where(inside[None], picked, 0.0).astype(np.float32)


def row_bands(table, height):
    spans = np.arange(height + 2 * HALF)[None, :] - np.arange(height)[:, None]
    inside = (spans >= 0) & (spans < KERNEL)
    picked = table[:, np.clip(spans, 0, KERNEL - 1)]
    return np.where(inside[None], picked, 0.0).astype(np.float32)


def coordinates(count, first, total):
    return (
        2.0 * (first + jnp.arange(count, dtype=jnp.int32)).astype(jnp.float32) + 1.0
    ) / total - 1.0


def solve_fit(gram, vector):
    regular = gram + RIDGE * jnp.diag(jnp.diag(gram))
    lower = jnp.linalg.cholesky(regular)
    return jax.scipy.linalg.cho_solve((lower, True), vector)


def shards(exposure, partners, offsets, stamps):
    visits = lax.axis_size("visit")
    tiles = lax.axis_size("tile")
    me = lax.axis_index("visit")
    my_tile = lax.axis_index("tile")
    image = exposure[0]
    height, width = image.shape
    block = height // visits
    chunks = -(-(width + 2 * HALF) // LANE)
    padded_width = chunks * LANE
    table = profile_table()

    blocks = image.reshape(visits, block, width)
    dest_rows = jnp.argmax(partners == me, axis=1).astype(jnp.int32)
    send = jnp.concatenate(
        [lax.dynamic_index_in_dim(blocks, dest_rows[v], 0, keepdims=True) for v in range(visits)]
    )
    recv = lax.all_to_all(send, "visit", 0, 0, tiled=True)

    left = HALF + SHIFT
    right = 2 * SHIFT + padded_width - left - width
    recv_p = jnp.pad(recv, ((0, 0), (0, 0), (left, right)))
    my_sources = partners[me]
    my_amounts = offsets[me]
    pieces = [
        lax.dynamic_slice(
            recv_p, (my_sources[r], 0, SHIFT + my_amounts[r]), (1, block, padded_width)
        )[0]
        for r in range(visits)
    ]
    columns = jnp.arange(padded_width, dtype=jnp.int32)
    keep = (columns >= HALF) & (columns < HALF + width)
    placed = jnp.where(keep[None, :], jnp.concatenate(pieces, axis=0), 0.0)

    forward = [(i, i + 1) for i in range(tiles - 1)]
    backward = [(i + 1, i) for i in range(tiles - 1)]
    above = lax.ppermute(placed[height - HALF :], "tile", forward)
    below = lax.ppermute(placed[:HALF], "tile", backward)
    field = jnp.concatenate([above, placed, below], axis=0)
    field_rows = height + 2 * HALF

    tiled = field.reshape(field_rows, chunks, LANE)
    windows = jnp.concatenate([tiled[:, : chunks - 1], tiled[:, 1:]], axis=-1)
    col_band = jnp.asarray(column_bands(table))
    filtered = [
        jnp.einsum("ybk,kx->ybx", windows, col_band[f], precision=HI).reshape(
            field_rows, (chunks - 1) * LANE
        )[:, :width]
        for f in range(len(SIGMA_LIST))
    ]

    row_band = jnp.asarray(row_bands(table, height))
    images = jnp.stack(
        [
            jnp.dot(row_band[ROW_PICK[k]], filtered[COLUMN_PICK[k]], precision=HI)
            for k in range(len(COLUMN_PICK))
        ]
    )
    nimg = images.shape[0]

    row_coord = coordinates(height, my_tile * height, height * tiles)
    col_coord = coordinates(width, 0, width)

    anchors = stamps[0, 0]
    nstamp = anchors.shape[0]
    cuts, science, stamp_rows, stamp_cols = [], [], [], []
    for s in range(nstamp):
        row_start = anchors[s, 0]
        col_start = anchors[s, 1]
        cuts.append(lax.dynamic_slice(images, (0, row_start, col_start), (nimg, STAMP, STAMP)))
        science.append(lax.dynamic_slice(image, (row_start, col_start), (STAMP, STAMP)))
        stamp_rows.append(lax.dynamic_slice_in_dim(row_coord, row_start, STAMP))
        stamp_cols.append(lax.dynamic_slice_in_dim(col_coord, col_start, STAMP))
    cut = jnp.stack(cuts)
    science = jnp.stack(science).reshape(nstamp, STAMP * STAMP)
    ry = jnp.stack(stamp_rows)[:, :, None]
    cx = jnp.stack(stamp_cols)[:, None, :]
    ones = jnp.ones((nstamp, STAMP, STAMP), jnp.float32)
    poly = jnp.stack([ones, ones * cx, ones * ry], axis=1)
    terms = (cut[:, :, None] * poly[:, None]).reshape(nstamp, 3 * nimg, STAMP * STAMP)
    design = jnp.concatenate([terms, poly.reshape(nstamp, 3, STAMP * STAMP)], axis=1)
    gram = jnp.einsum("sip,sjp->ij", design, design, precision=HI)
    vector = jnp.einsum("sip,sp->i", design, science, precision=HI)
    gram, vector = lax.psum((gram, vector), "tile")
    solution = solve_fit(gram, vector)

    weights = solution[: 3 * nimg].reshape(nimg, 3)
    cxf = col_coord[None, :]
    ryf = row_coord[:, None]
    model = solution[3 * nimg] + solution[3 * nimg + 1] * cxf + solution[3 * nimg + 2] * ryf
    for k in range(nimg):
        model = model + images[k] * (weights[k, 0] + weights[k, 1] * cxf + weights[k, 2] * ryf)
    difference = image - model
    return (difference[None], solution[None])


def solution(mesh):
    return jax.shard_map(
        shards,
        mesh=mesh,
        in_specs=(
            P(("groups", "visit"), "tile", None),
            P("groups", None),
            P("groups", None),
            P(("groups", "visit"), "tile", None, None),
        ),
        out_specs=(P(("groups", "visit"), "tile", None), P(("groups", "visit"), None)),
        check_vma=False,
    )
```

time: 925 us -> 336 us (0.36)
  local copies, waits for them, and re-layouts: 275 us -> 80.7 us
  loops' own time: 146 us -> 0 us
  waiting for transfers between devices: 137 us -> 0.01 us
  matrix products: 198 us -> 109 us
  other arithmetic: 141 us -> 53.7 us
  between operations: 14.3 us -> 71.4 us
    another operation x4 -> x0, loops' own time: 146 us -> none  [the longest x1 91.6 us: shards(): lax.map(image_block, jnp.arange(row_blocks * col_blocks, dtype=jnp.int32))]
    gather x72 -> x0, local copies, waits for them, and re-layouts: 145 us -> none  [the longest x4 89.5 us: band(): return jnp.where(inside[None], chosen[:, clipped], 0.0)]
    all_gather x1 -> x0, waiting for transfers between devices: 135 us -> none  [shards(): piece = lax.all_gather(blocks[None], 'visit', axis=0, tiled=True)]
    dot_general x96 -> x18, matrix products: 198 us -> 109 us  [the longest x10 49 us: shards(): jnp.dot(row_band[ROW_PICK[k]], filtered[COLUMN_PICK[k]], precision=HI)]
    add x72 -> x11, other arithmetic: 85 us -> 13.8 us  [the longest x10 12.6 us: shards(): weights[k, 0] + weights[k, 1] * cxf + weights[k, 2] * ryf]
    dynamic_slice x136 -> x2, local copies, waits for them, and re-layouts: 65.7 us -> 2.26 us  [the longest x1 1.55 us: shards(): lax.dynamic_slice(image, (row_start, col_start), (STAMP, STAMP))]
    mul x0 -> x2, local copies, waits for them, and re-layouts: none -> 32.6 us  [shards(): cut[:, :, None] * poly[:, None]]
    slice x73 -> x10, local copies, waits for them, and re-layouts: 33.2 us -> 5.27 us  [the longest x1 0.72 us: shards(): col_start = anchors[s, 1]]
  transfers between devices with their start and end apart: 3 -> 3, of which waited for: 2 -> 0; matrix products, arithmetic and copies ran while one was open for 11% -> 4% of each run, Pallas kernels for 0% -> 0%
where the time goes in v1:
time: 336 us; the launch traced here: 329 us
  matrix products  109 us (32%)
  local copies, waits for them, and re-layouts  80.7 us (24%)
  between operations  71.4 us (21%)
  other arithmetic  53.7 us (16%)
  starting transfers between devices  10 us (3%)
  blocking collectives  4.39 us (1%)
    dot_general x10, matrix products, shards(): jnp.dot(row_band[ROW_PICK[k]], filtered[COLUMN_PICK[k]], precision=HI)  49 us
    mul x2, local copies, waits for them, and re-layouts, shards(): cut[:, :, None] * poly[:, None]  32.6 us
    unnamed x77, local copies, waits for them, and re-layouts  27.1 us
    dot_general x6, matrix products, shards(): jnp.einsum('ybk,kx->ybx', windows, col_band[f], precision=HI)  24.4 us
    dot_general x1, matrix products, shards(): gram = jnp.einsum('sip,sjp->ij', design, design, precision=HI)  17.7 us
    dot_general x1, matrix products, shards(): vector = jnp.einsum('sip,sp->i', design, science, precision=HI)  17.4 us
    add x10, other arithmetic, shards(): weights[k, 0] + weights[k, 1] * cxf + weights[k, 2] * ryf  12.6 us
    broadcast_in_dim x1, other arithmetic, shards(): return (difference[None], solution[None])  11 us
  transfers between devices with their start and end apart: 3, of which 0 were waited for; matrix products, arithmetic and copies ran while one was open for 4% of the time, Pallas kernels for 0%

profile of v1, /device:TPU:0, one launch (start us, length us, event | category | flops | bytes accessed | tf_op | source)
XLA Modules:
  0.0 329.0 jit_solution(14863973612678887863)
XLA Ops:
  13.4 1.7 dynamic-slice_dynamic-update-slice_fusion.7
  15.6 1.7 dynamic-slice_dynamic-update-slice_fusion.6
  17.9 1.7 dynamic-slice_dynamic-update-slice_fusion.5
  20.2 1.7 dynamic-slice_dynamic-update-slice_fusion.4
  27.4 7.3 %all-to-all-start = ((f32[8,32,2048]{2,1,0:T(8,128)}), f32[8,32,2048]{2,1,0:T(8,128)S(1)}, u32[]{:S(2)}, u32[]{:S(2)}) async-start(f32[8,32,2048]{2,1,0:T(8,128)} %dynamic-slice_dynamic-update-slice_fusion), calls=%async_computation | async-start | bytes 4194304 | tf_op jit(solution)/shard_map/all_to_all | solution.py:75
  102.7 3.9 %copy.10 = f32[8,3,16384]{2,1,0:T(4,128)} copy(f32[8,3,16384]{2,0,1:T(8,128)} %reshape.294) | data formatting | bytes 3145728 | tf_op jit(solution)/shard_map/reshape | solution.py:138
  109.8 3.0 reshape.287
  113.8 4.0 %fusion.9 = f32[286,16,128]{2,1,0:T(8,128)S(1)} fusion(f32[256,128,1]{1,0,2:T(8,128)S(1)} %copy-done.19, f32[286,16,128]{2,1,0:T(8,128)S(1)} %get-tuple-element.7, f32[286,16,128]{2,1,0:T(8,128)S(1)} %get-tuple-element.6), kind=kOutput, calls=%fused_computation.44 | convolution fusion | flops 1800527872 | bytes 7159808 | tf_op jit(solution)/shard_map/ybk,kx->ybx/dot_general | solution.py:103
  119.0 4.0 %fusion.10 = f32[286,16,128]{2,1,0:T(8,128)S(1)} fusion(f32[256,128,1]{1,0,2:T(8,128)S(1)} %copy-done.18, f32[286,16,128]{2,1,0:T(8,128)S(1)} %get-tuple-element.7, f32[286,16,128]{2,1,0:T(8,128)S(1)} %get-tuple-element.6), kind=kOutput, calls=%fused_computation.45 | convolution fusion | flops 1800527872 | bytes 7159808 | tf_op jit(solution)/shard_map/ybk,kx->ybx/dot_general | solution.py:103
  124.2 4.2 %fusion.8 = f32[286,16,128]{2,1,0:T(8,128)S(1)} fusion(f32[256,128,1]{1,0,2:T(8,128)S(1)} %copy-done.17, f32[286,16,128]{2,1,0:T(8,128)S(1)} %get-tuple-element.7, f32[286,16,128]{2,1,0:T(8,128)S(1)} %get-tuple-element.6), kind=kOutput, calls=%fused_computation.43 | convolution fusion | flops 1800527872 | bytes 7159808 | tf_op jit(solution)/shard_map/ybk,kx->ybx/dot_general | solution.py:103
  129.7 4.8 %bitcast_dynamic-update-slice_fusion.9 = (f32[10,256,2048]{2,1,0:T(8,128)S(1)}, f32[256,2048]{1,0:T(8,128)}) fusion(f32[256,286]{1,0:T(8,128)S(1)} %copy-done.7, f32[286,2048]{1,0:T(8,128)S(1)} %bitcast.283), kind=kOutput, calls=%fused_computation.24 | convolution fusion | flops 1799356416 | bytes 6830080 | tf_op jit(solution)/shard_map/dot_general | solution.py:112
  134.5 4.8 %bitcast_dynamic-update-slice_fusion.8 = (f32[10,256,2048]{2,1,0:T(8,128)S(1)}, f32[256,2048]{1,0:T(8,128)}) fusion(f32[10,256,2048]{2,1,0:T(8,128)S(1)} %get-tuple-element.107, f32[256,286]{1,0:T(8,128)S(1)} %copy-done.7, f32[286,2048]{1,0:T(8,128)S(1)} %bitcast.288), kind=kOutput, calls=%fused_computation.23 | convolution fusion | flops 1799356416 | bytes 6946816 | tf_op jit(solution)/shard_map/dot_general | solution.py:112
  139.3 5.0 %bitcast_dynamic-update-slice_fusion.7 = (f32[10,256,2048]{2,1,0:T(8,128)S(1)}, f32[256,2048]{1,0:T(8,128)}) fusion(f32[10,256,2048]{2,1,0:T(8,128)S(1)} %get-tuple-element.109, f32[256,286]{1,0:T(8,128)S(1)} %copy-done.10, f32[286,2048]{1,0:T(8,128)S(1)} %bitcast.284), kind=kOutput, calls=%fused_computation.22 | convolution fusion | flops 1799356416 | bytes 6946816 | tf_op jit(solution)/shard_map/dot_general | solution.py:112
  144.4 4.9 %bitcast_dynamic-update-slice_fusion.6 = (f32[10,256,2048]{2,1,0:T(8,128)S(1)}, f32[256,2048]{1,0:T(8,128)}) fusion(f32[10,256,2048]{2,1,0:T(8,128)S(1)} %get-tuple-element.111, f32[256,286]{1,0:T(8,128)S(1)} %copy-done.7, f32[286,2048]{1,0:T(8,128)S(1)} %bitcast.300), kind=kOutput, calls=%fused_computation.21 | convolution fusion | flops 1799356416 | bytes 6946816 | tf_op jit(solution)/shard_map/dot_general | solution.py:112
  149.2 4.8 %bitcast_dynamic-update-slice_fusion.5 = (f32[10,256,2048]{2,1,0:T(8,128)S(1)}, f32[256,2048]{1,0:T(8,128)}) fusion(f32[10,256,2048]{2,1,0:T(8,128)S(1)} %get-tuple-element.113, f32[256,286]{1,0:T(8,128)S(1)} %copy-done.10, f32[286,2048]{1,0:T(8,128)S(1)} %bitcast.289), kind=kOutput, calls=%fused_computation.20 | convolution fusion | flops 1799356416 | bytes 6946816 | tf_op jit(solution)/shard_map/dot_general | solution.py:112
  154.0 4.0 %fusion.7 = f32[286,16,128]{2,1,0:T(8,128)S(1)} fusion(f32[256,128,1]{1,0,2:T(8,128)S(1)} %copy-done.16, f32[286,16,128]{2,1,0:T(8,128)S(1)} %get-tuple-element.7, f32[286,16,128]{2,1,0:T(8,128)S(1)} %get-tuple-element.6), kind=kOutput, calls=%fused_computation.42 | convolution fusion | flops 1800527872 | bytes 7159808 | tf_op jit(solution)/shard_map/ybk,kx->ybx/dot_general | solution.py:103
  159.7 4.0 %fusion.6 = f32[286,16,128]{2,1,0:T(8,128)S(1)} fusion(f32[256,128,1]{1,0,2:T(8,128)S(1)} %copy-done.15, f32[286,16,128]{2,1,0:T(8,128)S(1)} %get-tuple-element.7, f32[286,16,128]{2,1,0:T(8,128)S(1)} %get-tuple-element.6), kind=kOutput, calls=%fused_computation.41 | convolution fusion | flops 1800527872 | bytes 7159808 | tf_op jit(solution)/shard_map/ybk,kx->ybx/dot_general | solution.py:103
  164.9 4.0 %fusion.5 = f32[286,16,128]{2,1,0:T(8,128)S(1)} fusion(f32[256,128,1]{1,0,2:T(8,128)S(1)} %copy-done.14, f32[286,16,128]{2,1,0:T(8,128)S(1)} %get-tuple-element.7, f32[286,16,128]{2,1,0:T(8,128)S(1)} %get-tuple-element.6), kind=kOutput, calls=%fused_computation.40 | convolution fusion | flops 1800527872 | bytes 7159808 | tf_op jit(solution)/shard_map/ybk,kx->ybx/dot_general | solution.py:103
  170.2 5.1 %bitcast_dynamic-update-slice_fusion.4 = (f32[10,256,2048]{2,1,0:T(8,128)S(1)}, f32[256,2048]{1,0:T(8,128)}) fusion(f32[10,256,2048]{2,1,0:T(8,128)S(1)} %get-tuple-element.115, f32[256,286]{1,0:T(8,128)S(1)} %copy-done.13, f32[286,2048]{1,0:T(8,128)S(1)} %bitcast.285), kind=kOutput, calls=%fused_computation.19 | convolution fusion | flops 1799356416 | bytes 6946816 | tf_op jit(solution)/shard_map/dot_general | solution.py:112
  175.2 4.9 %bitcast_dynamic-update-slice_fusion.3 = (f32[10,256,2048]{2,1,0:T(8,128)S(1)}, f32[256,2048]{1,0:T(8,128)}) fusion(f32[10,256,2048]{2,1,0:T(8,128)S(1)} %get-tuple-element.117, f32[256,286]{1,0:T(8,128)S(1)} %copy-done.9, f32[286,2048]{1,0:T(8,128)S(1)} %bitcast.286), kind=kOutput, calls=%fused_computation.18 | convolution fusion | flops 1799356416 | bytes 6946816 | tf_op jit(solution)/shard_map/dot_general | solution.py:112
  180.1 4.8 %bitcast_dynamic-update-slice_fusion.2 = (f32[10,256,2048]{2,1,0:T(8,128)S(1)}, f32[256,2048]{1,0:T(8,128)}) fusion(f32[10,256,2048]{2,1,0:T(8,128)S(1)} %get-tuple-element.119, f32[256,286]{1,0:T(8,128)S(1)} %copy-done.9, f32[286,2048]{1,0:T(8,128)S(1)} %bitcast.299), kind=kOutput, calls=%fused_computation.17 | convolution fusion | flops 1799356416 | bytes 6946816 | tf_op jit(solution)/shard_map/dot_general | solution.py:112
  184.9 4.9 %bitcast_dynamic-update-slice_fusion.1 = (f32[10,256,2048]{2,1,0:T(8,128)S(1)}, f32[256,2048]{1,0:T(8,128)}) fusion(f32[10,256,2048]{2,1,0:T(8,128)S(1)} %get-tuple-element.121, f32[256,286]{1,0:T(8,128)S(1)} %copy-done.12, f32[286,2048]{1,0:T(8,128)S(1)} %bitcast.287), kind=kOutput, calls=%fused_computation.16 | convolution fusion | flops 1799356416 | bytes 6946816 | tf_op jit(solution)/shard_map/dot_general | solution.py:112
  189.8 5.1 %bitcast_dynamic-update-slice_fusion = (f32[10,256,2048]{2,1,0:T(8,128)S(1)}, f32[256,2048]{1,0:T(8,128)}) fusion(f32[10,256,2048]{2,1,0:T(8,128)S(1)} %get-tuple-element.123, f32[256,286]{1,0:T(8,128)S(1)} %copy-done.11, f32[286,2048]{1,0:T(8,128)S(1)} %bitcast.298), kind=kOutput, calls=%fused_computation.15 | convolution fusion | flops 1799356416 | bytes 6946816 | tf_op jit(solution)/shard_map/dot_general | solution.py:112
  203.8 10.4 %broadcast_multiply_fusion = f32[8,10,3,128,128]{4,3,0,2,1:T(8,128)} fusion(f32[8,3,128,128]{3,2,0,1:T(8,128)S(1)} %copy-done.1, f32[8,10,128,128]{3,2,0,1:T(8,128)} %bitcast_dynamic-update-slice_fusion.10), kind=kLoop, calls=%fused_computation.4 | loop fusion | flops 3932160 | bytes 22544384 | tf_op jit(solution)/shard_map/mul | solution.py:137
  214.2 17.9 %mul.428 = f32[8,30,16384]{2,0,1:T(8,128)} reshape(f32[8,10,3,128,128]{4,3,0,2,1:T(8,128)} %broadcast_multiply_fusion) | data formatting | bytes 31457280 | tf_op jit(solution)/shard_map/mul | solution.py:137
  232.1 14.7 %copy.9 = f32[8,30,16384]{2,1,0:T(8,128)S(1)} copy(f32[8,30,16384]{2,0,1:T(8,128)} %mul.428) | data formatting | bytes 31457280 | tf_op jit(solution)/shard_map/mul | solution.py:137
  246.8 17.7 %fusion.3 = f32[33,33]{1,0:T(8,128)S(1)} fusion(f32[8,3,16384]{2,1,0:T(4,128)S(1)} %copy-done.6, f32[8,30,16384]{2,1,0:T(8,128)S(1)} %copy.9), kind=kOutput, calls=%fused_computation.29 | convolution fusion | flops 1717174272 | bytes 17305860 | tf_op jit(solution)/shard_map/sip,sjp->ij/dot_general | solution.py:139
  264.5 17.4 %fusion.4 = f32[33]{0:T(128)S(1)} fusion(f32[8,3,16384]{2,1,0:T(4,128)S(1)} %copy-done.6, f32[8,30,16384]{2,1,0:T(8,128)S(1)} %copy.9, f32[8,16384,1]{1,0,2:T(8,128)S(1)} %bitcast.307), kind=kOutput, calls=%fused_computation.30 | convolution fusion | flops 56229888 | bytes 17825924 | tf_op jit(solution)/shard_map/sip,sp->i/dot_general | solution.py:140
  282.0 4.4 %all-reduce.1 = (f32[33,33]{1,0:T(8,128)S(1)}, f32[33]{0:T(128)S(1)}) all-reduce(f32[33,33]{1,0:T(8,128)S(1)} %fusion.3, f32[33]{0:T(128)S(1)} %fusion.4), channel_id=1, replica_groups=mesh['groups'=2,'visit'=8,'tile'=2] {'tile'}, use_global_device_ids=true, to_apply=%region_1.2 | all-reduce | flops 1122 | bytes 8976 | tf_op jit(solution)/shard_map/psum | solution.py:141
  287.6 3.0 cholesky.16
  291.9 2.5 custom-call.10
  317.6 11.0 %fusion.2 = f32[1,256,2048]{2,1,0:T(8,128)} fusion(f32[1,256,2048]{2,1,0:T(8,128)S(1)} %copy-done.3, f32[256,2048]{1,0:T(8,128)} %get-tuple-element.126, f32[256,2048]{1,0:T(8,128)} %get-tuple-element.124, f32[256,2048]{1,0:T(8,128)} %get-tuple-element.122, f32[256,2048]{1,0:T(8,128)} %get-tuple-element.120, f32[256,2048]{1,0:T(8,128)} %get-tuple-element.118, ...), kind=kLoop, calls=%fused_computation.26 | loop fusion | flops 16777216 | bytes 25267200 | tf_op jit(solution)/shard_map/broadcast_in_dim | solution.py:151
  (141 shorter events, 64.2 us)
Async XLA Ops:
  0.6 21.8 %copy-start.2 = (f32[1,256,2048]{2,1,0:T(8,128)S(1)}, f32[1,256,2048]{2,1,0:T(8,128)}, u32[]{:S(2)}) copy-start(f32[1,256,2048]{2,1,0:T(8,128)} %param.6) | copy-start | bytes 6291460
  26.6 29.8 %copy-start.20 = (s32[1,1,8,2]{2,3,1,0:T(2,128)S(1)}, s32[1,1,8,2]{2,3,1,0:T(2,128)}, u32[]{:S(2)}) copy-start(s32[1,1,8,2]{2,3,1,0:T(2,128)} %param.9) | copy-start | bytes 196
  27.4 66.8 %all-to-all-start = ((f32[8,32,2048]{2,1,0:T(8,128)}), f32[8,32,2048]{2,1,0:T(8,128)S(1)}, u32[]{:S(2)}, u32[]{:S(2)}) async-start(f32[8,32,2048]{2,1,0:T(8,128)} %dynamic-slice_dynamic-update-slice_fusion), calls=%async_computation | async-start | bytes 4194304 | tf_op jit(solution)/shard_map/all_to_all | solution.py:75
  95.4 5.9 %copy-start = (f32[8,3,128,128]{3,2,0,1:T(8,128)S(1)}, f32[8,3,128,128]{3,2,0,1:T(8,128)}, u32[]{:S(2)}) copy-start(f32[8,3,128,128]{3,2,0,1:T(8,128)} %pad_maximum_fusion.5) | copy-start | bytes 4718596
  95.5 1.4 copy-start.4
  97.0 11.2 %collective-permute-start = (f32[15,2176]{1,0:T(8,128)S(1)}, f32[15,2176]{1,0:T(8,128)S(1)}, u32[]{:S(2)}, u32[]{:S(2)}) collective-permute-start(f32[15,2176]{1,0:T(8,128)S(1)} %get-tuple-element.8), channel_id=1, source_target_pairs={{0,1},{2,3},{4,5},{6,7},{8,9},{10,11},{12,13},{14,15},{16,17},{18,... | collective-permute-start | bytes 391688 | tf_op jit(solution)/shard_map/ppermute | solution.py:94
  98.4 9.7 %collective-permute-start.1 = (f32[15,2176]{1,0:T(8,128)S(1)}, f32[15,2176]{1,0:T(8,128)S(1)}, u32[]{:S(2)}, u32[]{:S(2)}) collective-permute-start(f32[15,2176]{1,0:T(8,128)S(1)} %get-tuple-element.9), channel_id=1, source_target_pairs={{1,0},{3,2},{5,4},{7,6},{9,8},{11,10},{13,12},{15,14},{17,16},{19,... | collective-permute-start | bytes 391688 | tf_op jit(solution)/shard_map/ppermute | solution.py:95
  102.7 5.4 %copy-start.5 = (f32[256,2176]{1,0:T(8,128)S(1)}, f32[256,2176]{1,0:T(8,128)}, u32[]{:S(2)}) copy-start(f32[256,2176]{1,0:T(8,128)} %copy-done.4) | copy-start | bytes 6684676
  112.8 0.9 copy-start.19
  118.0 1.0 copy-start.18
  123.2 1.0 copy-start.17
  128.6 1.0 copy-start.7
  134.5 4.8 %copy-start.10 = (f32[256,286]{1,0:T(8,128)S(1)}, f32[256,286]{1,0:T(8,128)}, u32[]{:S(2)}) copy-start(f32[256,286]{1,0:T(8,128)} %constant.173) | copy-start | bytes 878596
  149.2 4.8 %copy-start.16 = (f32[256,128,1]{1,0,2:T(8,128)S(1)}, f32[256,128,1]{1,0,2:T(8,128)}, u32[]{:S(2)}) copy-start(f32[256,128,1]{1,0,2:T(8,128)} %constant.206) | copy-start | bytes 393220
  158.2 1.4 copy-start.15
  163.9 1.0 copy-start.14
  169.1 1.0 copy-start.13
  170.2 5.1 %copy-start.9 = (f32[256,286]{1,0:T(8,128)S(1)}, f32[256,286]{1,0:T(8,128)}, u32[]{:S(2)}) copy-start(f32[256,286]{1,0:T(8,128)} %constant.179) | copy-start | bytes 878596
  180.1 4.8 %copy-start.12 = (f32[256,286]{1,0:T(8,128)S(1)}, f32[256,286]{1,0:T(8,128)}, u32[]{:S(2)}) copy-start(f32[256,286]{1,0:T(8,128)} %constant.185) | copy-start | bytes 878596
  184.9 4.9 %copy-start.11 = (f32[256,286]{1,0:T(8,128)S(1)}, f32[256,286]{1,0:T(8,128)}, u32[]{:S(2)}) copy-start(f32[256,286]{1,0:T(8,128)} %constant.187) | copy-start | bytes 878596
  199.3 4.5 %copy-start.1 = (f32[8,3,128,128]{3,2,0,1:T(8,128)S(1)}, f32[8,3,128,128]{3,2,0,1:T(8,128)}, u32[]{:S(2)}) copy-start(f32[8,3,128,128]{3,2,0,1:T(8,128)} %pad_maximum_fusion.5) | copy-start | bytes 4718596
  232.1 14.7 %copy-start.6 = (f32[8,3,16384]{2,1,0:T(4,128)S(1)}, f32[8,3,16384]{2,1,0:T(4,128)}, u32[]{:S(2)}) copy-start(f32[8,3,16384]{2,1,0:T(4,128)} %copy.10) | copy-start | bytes 4718596
  246.8 17.7 %copy-start.8 = (f32[8,16384]{1,0:T(8,128)S(1)}, f32[8,16384]{1,0:T(8,128)}, u32[]{:S(2)}) copy-start(f32[8,16384]{1,0:T(8,128)} %stack.199) | copy-start | bytes 1572868
  264.5 53.0 %copy-start.3 = (f32[1,256,2048]{2,1,0:T(8,128)S(1)}, f32[1,256,2048]{2,1,0:T(8,128)}, u32[]{:S(2)}) copy-start(f32[1,256,2048]{2,1,0:T(8,128)} %param.6) | copy-start | bytes 6291460
  294.7 33.8 %copy-start.21 = (f32[1,33]{1,0:T(1,128)}, f32[1,33]{1,0:T(1,128)S(1)}, u32[]{:S(2)}) copy-start(f32[1,33]{1,0:T(1,128)S(1)} %fusion.29) | copy-start | bytes 400
